TPU v7x, 32 devices: a whole 2x2x4 slice. The times are simulated.
32 devices in a mesh: grp: 8 (over z, x), leaf: 4 (over y, core).
Axes of the slice: x: 2, y: 2, z: 4, core: 2. Of those that a mesh axis runs over, the one named last changes fastest.
Arguments:
- inputs: float32 [65536, 64], P(('grp', 'leaf')), may hold values from -6 to 6
- freqs: float32 [64, 256], replicated, may hold values from -0.75 to 0.75
- phases: float32 [256], replicated, may hold values from -3.140625 to 3.140625
- sample_weight: float32 [65536], P(('grp', 'leaf')), as said below
- stored: float32 [32, 256, 256], P(('grp', 'leaf')), as said below
- root: int32 [32], replicated, may hold values from 0 to 31, each once
Outputs:
- factor: float32 [256, 256], replicated
- basis: float32 [65536, 256], P(('grp', 'leaf'))
Inputs may be any that keep to these rules, and one draw needn't show every extreme that they name: `root`: each device index once, in the order grp first, leaf second; only the first entry is read. `stored`: each slot is upper triangular with a positive diagonal. `sample_weight`: positive row weights.
All inputs are finite; a program needn't handle non-finite values.
Results may differ from a plain program's by a relative error of at most 0.0003.
Values sent between devices are 32-bit elements; how exact they have to be, the bound alone decides.
No kernel may reach another device: no remote copies, remote signals or barrier semaphores. Data moves between devices by JAX's collectives and lax.ppermute only.
A program may use at most 64 MiB of HBM per device.

v0:
```python
import math
import jax
import jax.numpy as jnp
from jax import lax
from jax.sharding import PartitionSpec as P


def partner(array, axis, distance):
    return lax.ppermute(array, axis, [(i, i ^ 1 << distance) for i in range(lax.axis_size(axis))])


def spread(array, axis, root):
    mine = lax.axis_index(axis) == root
    return lax.psum(jnp.where(mine, array, jnp.zeros_like(array)), axis)


def per_device(inputs, freqs, phases, sample_weight, stored, root):
    total_rows = inputs.shape[0] * lax.axis_size("grp") * lax.axis_size("leaf")
    norm_scale = 1.0 / math.sqrt(total_rows)
    proj = jnp.dot(inputs, freqs, precision=lax.Precision.HIGHEST) + phases[None, :]
    features = jnp.sqrt(sample_weight)[:, None] * jnp.cos(proj) * norm_scale
    gram = lax.dot_general(
        features, features, (((0,), (0,)), ((), ())), precision=lax.Precision.HIGHEST
    )
    running = stored[0]
    payload = gram
    for bit_leaf in range(lax.axis_size("leaf").bit_length() - 1):
        payload = payload + partner(payload, "leaf", bit_leaf)
    for bit_grp in range(lax.axis_size("grp").bit_length() - 1):
        payload = payload + partner(payload, "grp", bit_grp)
    gram = payload
    carried = spread(running, ("grp", "leaf"), root[0])
    gram = jnp.dot(carried.T, carried, precision=lax.Precision.HIGHEST) + gram
    lower = jnp.linalg.cholesky(gram)
    solved = jax.scipy.linalg.solve_triangular(lower, features.T, lower=True)
    basis = solved.T * math.sqrt(total_rows)
    return (lower.T, basis)


def solution(mesh):
    return jax.shard_map(
        per_device,
        mesh=mesh,
        in_specs=(
            P(("grp", "leaf"), None),
            P(),
            P(),
            P(("grp", "leaf")),
            P(("grp", "leaf"), None, None),
            P(),
        ),
        out_specs=(P(), P(("grp", "leaf"), None)),
        check_vma=False,
    )
```

profile of v0, /device:TPU:0, one launch (start us, length us, event | category | flops | bytes accessed | tf_op | source)
XLA Modules:
  0.0 246.1 jit_solution(17475438517466494014)
XLA Ops:
  8.2 9.5 %fusion.2 = f32[2048,256]{1,0:T(8,128)S(1)} fusion(f32[2048,64]{0,1:T(8,128)S(1)} %copy-done, f32[64,256]{1,0:T(8,128)} %param.7, f32[256]{0:T(256)} %param.8, f32[2048]{0:T(1024)S(1)} %sqrt.3), kind=kOutput, calls=%fused_computation.5 | convolution fusion | flops 404226048 | bytes 2696192 | tf_op jit(solution)/shard_map/dot_general | solution.py:20
  17.8 3.6 %fusion.16 = f32[256,256]{0,1:T(8,128)S(1)} fusion(f32[2048,256]{1,0:T(8,128)S(1)} %fusion.2), kind=kOutput, calls=%fused_computation.39 | convolution fusion | flops 1610612736 | bytes 2359296 | tf_op jit(solution)/shard_map/dot_general | solution.py:22
  22.0 1.2 collective-permute-done
  23.2 2.9 %collective-permute-start.1 = (f32[256,256]{0,1:T(8,128)S(1)}, f32[256,256]{0,1:T(8,128)S(1)}, u32[]{:S(2)}, u32[]{:S(2)}) collective-permute-start(f32[256,256]{0,1:T(8,128)S(1)} %add.59), channel_id=1, source_target_pairs={{0,2},{1,3},{2,0},{3,1},{4,6},{5,7},{6,4},{7,5},{8,10},{9,11},{10,... | collective-permute-start | bytes 786440 | tf_op jit(solution)/shard_map/ppermute | solution.py:9
  26.1 6.6 %collective-permute-done.1 = f32[256,256]{0,1:T(8,128)S(1)} collective-permute-done((f32[256,256]{0,1:T(8,128)S(1)}, f32[256,256]{0,1:T(8,128)S(1)}, u32[]{:S(2)}, u32[]{:S(2)}) %collective-permute-start.1) | collective-permute-done | bytes 262176 | tf_op jit(solution)/shard_map/ppermute | solution.py:9
  32.8 1.8 collective-permute-start.2
  34.6 6.1 %collective-permute-done.2 = f32[256,256]{0,1:T(8,128)S(1)} collective-permute-done((f32[256,256]{0,1:T(8,128)S(1)}, f32[256,256]{0,1:T(8,128)S(1)}, u32[]{:S(2)}, u32[]{:S(2)}) %collective-permute-start.2) | collective-permute-done | bytes 262176 | tf_op jit(solution)/shard_map/ppermute | solution.py:9
  40.6 1.6 collective-permute-start.3
  43.0 4.6 %collective-permute-done.3 = f32[256,256]{0,1:T(8,128)S(1)} collective-permute-done((f32[256,256]{0,1:T(8,128)S(1)}, f32[256,256]{0,1:T(8,128)S(1)}, u32[]{:S(2)}, u32[]{:S(2)}) %collective-permute-start.3) | collective-permute-done | bytes 262176 | tf_op jit(solution)/shard_map/ppermute | solution.py:9
  47.7 2.3 collective-permute-start.4
  50.0 121.1 %all-reduce.3.cloned.1.call-done = f32[256,256]{1,0:T(8,128)} async-done(((f32[256,256]{1,0:T(8,128)}), f32[256,256]{1,0:T(8,128)}) %all-reduce.3.cloned.1.call-update) | async-done | bytes 262160 | tf_op jit(solution)/shard_map/psum | solution.py:14
  171.1 1.6 fusion.15
  173.0 11.7 %cholesky.49 = f32[128,128]{1,0:T(8,128)S(1)} custom-call(f32[128,128]{1,0:T(8,128)S(1)} %cholesky.115), custom_call_target="Cholesky" | custom-call | tf_op jit(solution)/shard_map/jit(cholesky)/cholesky | solution.py:34
  184.7 9.8 %custom-call.15 = f32[1,128,128]{1,2,0:T(8,128)S(1)} custom-call(f32[1,128,128]{2,1,0:T(8,128)S(1)} %get-tuple-element.27), custom_call_target="InvertDiagBlocksLowerTriangular" | custom-call | tf_op jit(solution)/shard_map/jit(cholesky)/cholesky | solution.py:34
  195.1 11.7 %cholesky.103 = f32[128,128]{1,0:T(8,128)S(1)} custom-call(f32[128,128]{1,0:T(8,128)S(1)} %convolution_subtract_fusion.1), custom_call_target="Cholesky" | custom-call | tf_op jit(solution)/shard_map/jit(cholesky)/cholesky | solution.py:34
  208.8 0.8 copy.12
  209.7 3.9 %while.1 = (s32[]{:T(128)}, f32[256,256]{1,0:T(8,128)S(1)}, s32[2,2]{1,0:T(2,128)S(1)}, f32[2,128,128]{2,1,0:T(8,128)S(1)}, s32[]{:T(128)}) while((s32[]{:T(128)}, f32[256,256]{1,0:T(8,128)S(1)}, s32[2,2]{1,0:T(2,128)S(1)}, f32[2,128,128]{2,1,0:T(8,128)S(1)}, s32[]{:T(128)}) %tuple.29), condition=%wide.while_cond, body=%wide.while_body.sunk | while | flops 2 | bytes 131189 | solution.py:35
  210.3 1.3 bitcast_dynamic-update-slice_fusion.2
  212.3 1.3 bitcast_dynamic-update-slice_fusion.2
  213.6 19.7 %custom-call.16 = f32[2,128,128]{1,2,0:T(8,128)S(1)} custom-call(f32[2,128,128]{2,1,0:T(8,128)S(1)} %get-tuple-element.9), custom_call_target="InvertDiagBlocksLowerTriangular" | custom-call | tf_op jit(solution)/shard_map/jit(_solve_triangular)/triangular_solve | solution.py:35
  233.3 1.1 fusion.4
  234.4 1.8 convolution_subtract_fusion
  236.2 1.1 fusion.10
  237.5 1.8 copy.13
  (35 shorter events, 5.4 us)
Async XLA Ops:
  7.2 1.1 copy-start
  7.2 163.9 %all-reduce.3.cloned.1.call-start = ((), (), s32[]{:S(2)}) async-start(), calls=%async_computation | async-start | bytes 524288 | tf_op jit(solution)/shard_map/psum | solution.py:14
  21.4 20.8 %copy-start.2 = (s32[32]{0:T(128)S(1)}, s32[32]{0:T(128)}, u32[]{:S(2)}) copy-start(s32[32]{0:T(128)} %param.11) | copy-start | bytes 388
  21.4 20.9 %copy-start.1 = (f32[1,256,256]{2,1,0:T(8,128)S(1)}, f32[1,256,256]{2,1,0:T(8,128)}, u32[]{:S(2)}) copy-start(f32[1,256,256]{2,1,0:T(8,128)} %param.10) | copy-start | bytes 786436
  21.4 1.7 collective-permute-start
  23.2 9.5 %collective-permute-start.1 = (f32[256,256]{0,1:T(8,128)S(1)}, f32[256,256]{0,1:T(8,128)S(1)}, u32[]{:S(2)}, u32[]{:S(2)}) collective-permute-start(f32[256,256]{0,1:T(8,128)S(1)} %add.59), channel_id=1, source_target_pairs={{0,2},{1,3},{2,0},{3,1},{4,6},{5,7},{6,4},{7,5},{8,10},{9,11},{10,... | collective-permute-start | bytes 786440 | tf_op jit(solution)/shard_map/ppermute | solution.py:9
  32.8 7.8 %collective-permute-start.2 = (f32[256,256]{0,1:T(8,128)S(1)}, f32[256,256]{0,1:T(8,128)S(1)}, u32[]{:S(2)}, u32[]{:S(2)}) collective-permute-start(f32[256,256]{0,1:T(8,128)S(1)} %add.60), channel_id=1, source_target_pairs={{0,4},{4,0},{8,12},{12,8},{16,20},{20,16},{24,28},{28,24},{1,5},{5... | collective-permute-start | bytes 786440 | tf_op jit(solution)/shard_map/ppermute | solution.py:9
  40.6 7.0 %collective-permute-start.3 = (f32[256,256]{0,1:T(8,128)S(1)}, f32[256,256]{0,1:T(8,128)S(1)}, u32[]{:S(2)}, u32[]{:S(2)}) collective-permute-start(f32[256,256]{0,1:T(8,128)S(1)} %add.61), channel_id=1, source_target_pairs={{0,8},{4,12},{8,0},{12,4},{16,24},{20,28},{24,16},{28,20},{1,9},{5... | collective-permute-start | bytes 786440 | tf_op jit(solution)/shard_map/ppermute | solution.py:9
  47.7 125.1 %collective-permute-start.4 = (f32[256,256]{0,1:T(8,128)S(1)}, f32[256,256]{0,1:T(8,128)S(1)}, u32[]{:S(2)}, u32[]{:S(2)}) collective-permute-start(f32[256,256]{0,1:T(8,128)S(1)} %add.62), channel_id=1, source_target_pairs={{0,16},{4,20},{8,24},{12,28},{16,0},{20,4},{24,8},{28,12},{1,17},{... | collective-permute-start | bytes 786440 | tf_op jit(solution)/shard_map/ppermute | solution.py:9
Sparse Core Ops, SparseCore 0:
  43.2 127.8 all-reduce.2
where the time goes:
time: 246 us
  waiting for transfers between devices  140 us (57%)
  other arithmetic  54.8 us (22%)
  matrix products  19.2 us (8%)
  between operations  15.6 us (6%)
  starting transfers between devices  9.21 us (4%)
  local copies, waits for them, and re-layouts  7.77 us (3%)
    psum x1, waiting for transfers between devices, spread(): return lax.psum(jnp.where(mine, array, jnp.zeros_like(array)), axis)  121 us
    another operation x6, other arithmetic, per_device(): lower = jnp.linalg.cholesky(gram)  34 us
    another operation x3, other arithmetic, per_device(): solved = jax.scipy.linalg.solve_triangular(lower, features.T, lower=True)  19.7 us
    ppermute x5, waiting for transfers between devices, partner(): lax.ppermute(array, axis, [(i, i ^ 1 << distance) for i in range(lax.axis...  18.4 us
    dot_general x1, matrix products, per_device(): jnp.dot(inputs, freqs, precision=lax.Precision.HIGHEST) + phases[None, :]  9.54 us
    ppermute x5, starting transfers between devices, partner(): lax.ppermute(array, axis, [(i, i ^ 1 << distance) for i in range(lax.axis...  9.17 us
  transfers between devices with their start and end apart: 6, of which 5 were waited for; matrix products, arithmetic and copies ran while one was open for 1% of the time, Pallas kernels for 0%

commit v1 on v0

--- a/solution.py
+++ b/solution.py
@@ -11,7 +11,7 @@
 
 def spread(array, axis, root):
     mine = lax.axis_index(axis) == root
-    return lax.psum(jnp.where(mine, array, jnp.zeros_like(array)), axis)
+    return jnp.sum(lax.all_gather(jnp.where(mine, array, jnp.zeros_like(array)), axis), axis=0)
 
 
 def per_device(inputs, freqs, phases, sample_weight, stored, root):

time: 246 us -> 176 us (0.72)
  waiting for transfers between devices: 140 us -> 64.5 us
  other arithmetic: 54.8 us -> 58.9 us
    psum x1 -> x0, waiting for transfers between devices: 121 us -> none  [spread(): return lax.psum(jnp.where(mine, array, jnp.zeros_like(array)), axis)]
    all_gather x0 -> x1, waiting for transfers between devices: none -> 37.4 us  [spread(): lax.all_gather(jnp.where(mine, array, jnp.zeros_like(array)), axis)]
    ppermute x5, waiting for transfers between devices: 18.4 us -> 27.1 us  [partner(): lax.ppermute(array, axis, [(i, i ^ 1 << distance) for i in range(lax.axis...]
    reduce_sum x0 -> x1, other arithmetic: none -> 3.93 us  [spread(): jnp.sum(lax.all_gather(jnp.where(mine, array, jnp.zeros_like(array)), axi...]
  transfers between devices with their start and end apart: 6 -> 6, of which waited for: 5 -> 5; matrix products, arithmetic and copies ran while one was open for 1% -> 11% of each run, Pallas kernels for 0% -> 0%
where the time goes in v1:
time: 176 us; the launch traced here: 175 us
  waiting for transfers between devices  64.5 us (37%)
  other arithmetic  58.9 us (33%)
  matrix products  18.2 us (10%)
  between operations  16.2 us (9%)
  starting transfers between devices  9.96 us (6%)
  local copies, waits for them, and re-layouts  7.52 us (4%)
    all_gather x1, waiting for transfers between devices, spread(): lax.all_gather(jnp.where(mine, array, jnp.zeros_like(array)), axis)  37.4 us
    another operation x6, other arithmetic, per_device(): lower = jnp.linalg.cholesky(gram)  34.1 us
    ppermute x5, waiting for transfers between devices, partner(): lax.ppermute(array, axis, [(i, i ^ 1 << distance) for i in range(lax.axis...  27.1 us
    another operation x3, other arithmetic, per_device(): solved = jax.scipy.linalg.solve_triangular(lower, features.T, lower=True)  19.7 us
    ppermute x5, starting transfers between devices, partner(): lax.ppermute(array, axis, [(i, i ^ 1 << distance) for i in range(lax.axis...  9.92 us
    dot_general x1, matrix products, per_device(): jnp.dot(inputs, freqs, precision=lax.Precision.HIGHEST) + phases[None, :]  9.55 us
    another operation x3, matrix products, per_device(): solved = jax.scipy.linalg.solve_triangular(lower, features.T, lower=True)  3.96 us
    another operation x6, local copies, waits for them, and re-layouts  3.93 us
  transfers between devices with their start and end apart: 6, of which 5 were waited for; matrix products, arithmetic and copies ran while one was open for 11% of the time, Pallas kernels for 0%

profile of v1, /device:TPU:0, one launch (start us, length us, event | category | flops | bytes accessed | tf_op | source)
XLA Modules:
  0.0 175.3 jit_solution(15486323896641178968)
XLA Ops:
  9.4 9.5 %fusion.2 = f32[2048,256]{1,0:T(8,128)S(1)} fusion(f32[2048,64]{0,1:T(8,128)S(1)} %copy-done, f32[64,256]{1,0:T(8,128)} %param.7, f32[256]{0:T(256)} %param.8, f32[2048]{0:T(1024)S(1)} %sqrt.3), kind=kOutput, calls=%fused_computation.5 | convolution fusion | flops 404226048 | bytes 2696192 | tf_op jit(solution)/shard_map/dot_general | solution.py:20
  18.9 3.6 %fusion.16 = f32[256,256]{0,1:T(8,128)S(1)} fusion(f32[2048,256]{1,0:T(8,128)S(1)} %fusion.2), kind=kOutput, calls=%fused_computation.39 | convolution fusion | flops 1610612736 | bytes 2359296 | tf_op jit(solution)/shard_map/dot_general | solution.py:22
  23.1 1.2 collective-permute-done
  24.3 2.9 %collective-permute-start.1 = (f32[256,256]{0,1:T(8,128)S(1)}, f32[256,256]{0,1:T(8,128)S(1)}, u32[]{:S(2)}, u32[]{:S(2)}) collective-permute-start(f32[256,256]{0,1:T(8,128)S(1)} %add.57), channel_id=1, source_target_pairs={{0,2},{1,3},{2,0},{3,1},{4,6},{5,7},{6,4},{7,5},{8,10},{9,11},{10,... | collective-permute-start | bytes 786440 | tf_op jit(solution)/shard_map/ppermute | solution.py:9
  27.3 6.6 %collective-permute-done.1 = f32[256,256]{0,1:T(8,128)S(1)} collective-permute-done((f32[256,256]{0,1:T(8,128)S(1)}, f32[256,256]{0,1:T(8,128)S(1)}, u32[]{:S(2)}, u32[]{:S(2)}) %collective-permute-start.1) | collective-permute-done | bytes 262176 | tf_op jit(solution)/shard_map/ppermute | solution.py:9
  33.9 1.8 %collective-permute-start.2 = (f32[256,256]{0,1:T(8,128)S(1)}, f32[256,256]{0,1:T(8,128)S(1)}, u32[]{:S(2)}, u32[]{:S(2)}) collective-permute-start(f32[256,256]{0,1:T(8,128)S(1)} %add.58), channel_id=1, source_target_pairs={{0,4},{4,0},{8,12},{12,8},{16,20},{20,16},{24,28},{28,24},{1,5},{5... | collective-permute-start | bytes 786440 | tf_op jit(solution)/shard_map/ppermute | solution.py:9
  35.7 6.1 %collective-permute-done.2 = f32[256,256]{0,1:T(8,128)S(1)} collective-permute-done((f32[256,256]{0,1:T(8,128)S(1)}, f32[256,256]{0,1:T(8,128)S(1)}, u32[]{:S(2)}, u32[]{:S(2)}) %collective-permute-start.2) | collective-permute-done | bytes 262176 | tf_op jit(solution)/shard_map/ppermute | solution.py:9
  41.8 3.1 %collective-permute-start.3 = (f32[256,256]{0,1:T(8,128)S(1)}, f32[256,256]{0,1:T(8,128)S(1)}, u32[]{:S(2)}, u32[]{:S(2)}) collective-permute-start(f32[256,256]{0,1:T(8,128)S(1)} %add.59), channel_id=1, source_target_pairs={{0,8},{4,12},{8,0},{12,4},{16,24},{20,28},{24,16},{28,20},{1,9},{5... | collective-permute-start | bytes 786440 | tf_op jit(solution)/shard_map/ppermute | solution.py:9
  44.9 13.3 %collective-permute-done.3 = f32[256,256]{0,1:T(8,128)S(1)} collective-permute-done((f32[256,256]{0,1:T(8,128)S(1)}, f32[256,256]{0,1:T(8,128)S(1)}, u32[]{:S(2)}, u32[]{:S(2)}) %collective-permute-start.3) | collective-permute-done | bytes 262176 | tf_op jit(solution)/shard_map/ppermute | solution.py:9
  58.2 1.5 collective-permute-start.4
  59.7 37.4 %all-gather.2.cloned.1.call-done = f32[32,256,256]{2,1,0:T(8,128)} async-done(((f32[1,256,256]{2,1,0:T(8,128)}), f32[32,256,256]{2,1,0:T(8,128)}) %all-gather.2.cloned.1.call-update) | async-done | bytes 8388624 | tf_op jit(solution)/shard_map/all_gather | solution.py:14
  97.1 3.9 %reduce_sum.9 = f32[256,256]{1,0:T(8,128)S(1)} reduce(f32[32,256,256]{2,1,0:T(8,128)} %all-gather.2.cloned.1.call-done, f32[]{:T(128)} %constant.89.clone.1), dimensions={0}, to_apply=%region_0.1 | reduce | flops 2031616 | bytes 8650756 | tf_op jit(solution)/shard_map/reduce_sum | solution.py:14
  101.9 11.7 %cholesky.49 = f32[128,128]{1,0:T(8,128)S(1)} custom-call(f32[128,128]{1,0:T(8,128)S(1)} %cholesky.115), custom_call_target="Cholesky" | custom-call | tf_op jit(solution)/shard_map/jit(cholesky)/cholesky | solution.py:34
  113.7 9.8 %custom-call.15 = f32[1,128,128]{1,2,0:T(8,128)S(1)} custom-call(f32[1,128,128]{2,1,0:T(8,128)S(1)} %get-tuple-element.29), custom_call_target="InvertDiagBlocksLowerTriangular" | custom-call | tf_op jit(solution)/shard_map/jit(cholesky)/cholesky | solution.py:34
  124.0 11.9 %cholesky.103 = f32[128,128]{1,0:T(8,128)S(1)} custom-call(f32[128,128]{1,0:T(8,128)S(1)} %convolution_subtract_fusion.1), custom_call_target="Cholesky" | custom-call | tf_op jit(solution)/shard_map/jit(cholesky)/cholesky | solution.py:34
  137.9 0.8 copy.18
  138.8 4.0 %while.1 = (s32[]{:T(128)}, f32[256,256]{1,0:T(8,128)S(1)}, s32[2,2]{1,0:T(2,128)S(1)}, f32[2,128,128]{2,1,0:T(8,128)S(1)}, s32[]{:T(128)}) while((s32[]{:T(128)}, f32[256,256]{1,0:T(8,128)S(1)}, s32[2,2]{1,0:T(2,128)S(1)}, f32[2,128,128]{2,1,0:T(8,128)S(1)}, s32[]{:T(128)}) %tuple.30), condition=%wide.while_cond, body=%wide.while_body.sunk | while | flops 2 | bytes 131189 | solution.py:35
  139.4 1.4 bitcast_dynamic-update-slice_fusion.2
  141.4 1.4 bitcast_dynamic-update-slice_fusion.2
  142.8 19.7 %custom-call.16 = f32[2,128,128]{1,2,0:T(8,128)S(1)} custom-call(f32[2,128,128]{2,1,0:T(8,128)S(1)} %get-tuple-element.9), custom_call_target="InvertDiagBlocksLowerTriangular" | custom-call | tf_op jit(solution)/shard_map/jit(_solve_triangular)/triangular_solve | solution.py:35
  162.5 1.1 fusion.4
  163.5 1.8 %convolution_subtract_fusion = f32[128,2048]{0,1:T(8,128)S(1)} fusion(f32[128,2048]{1,0:T(8,128)S(1)} %fusion.4, f32[256,2048]{0,1:T(8,128)S(1)} %bitcast.45, f32[256,256]{1,0:T(8,128)S(1)} %get-tuple-element.80), kind=kOutput, calls=%fused_computation.6 | convolution fusion | flops 402915328 | bytes 3211264 | tf_op jit(solution)/shard_map/jit(_solve_triangular)/triangular_solve | solution.py:35
  165.4 1.1 fusion.10
  166.6 1.8 %copy.19 = f32[2048,256]{1,0:T(8,128)} copy(f32[2048,256]{0,1:T(8,128)S(1)} %fusion.3) | data formatting | bytes 4194304
  (32 shorter events, 5.7 us)
Async XLA Ops:
  7.2 2.2 %copy-start = (f32[2048,64]{0,1:T(8,128)S(1)}, f32[2048,64]{0,1:T(8,128)}, u32[]{:S(2)}) copy-start(f32[2048,64]{0,1:T(8,128)} %param.6) | copy-start | bytes 1572868
  7.2 89.9 %all-gather.2.cloned.1.call-start = ((), (), s32[]{:S(2)}) async-start(), calls=%async_computation | async-start | bytes 8650752 | tf_op jit(solution)/shard_map/all_gather | solution.py:14
  22.6 1.7 collective-permute-start
  24.3 9.6 %collective-permute-start.1 = (f32[256,256]{0,1:T(8,128)S(1)}, f32[256,256]{0,1:T(8,128)S(1)}, u32[]{:S(2)}, u32[]{:S(2)}) collective-permute-start(f32[256,256]{0,1:T(8,128)S(1)} %add.57), channel_id=1, source_target_pairs={{0,2},{1,3},{2,0},{3,1},{4,6},{5,7},{6,4},{7,5},{8,10},{9,11},{10,... | collective-permute-start | bytes 786440 | tf_op jit(solution)/shard_map/ppermute | solution.py:9
  33.9 7.8 %collective-permute-start.2 = (f32[256,256]{0,1:T(8,128)S(1)}, f32[256,256]{0,1:T(8,128)S(1)}, u32[]{:S(2)}, u32[]{:S(2)}) collective-permute-start(f32[256,256]{0,1:T(8,128)S(1)} %add.58), channel_id=1, source_target_pairs={{0,4},{4,0},{8,12},{12,8},{16,20},{20,16},{24,28},{28,24},{1,5},{5... | collective-permute-start | bytes 786440 | tf_op jit(solution)/shard_map/ppermute | solution.py:9
  41.8 16.4 %collective-permute-start.3 = (f32[256,256]{0,1:T(8,128)S(1)}, f32[256,256]{0,1:T(8,128)S(1)}, u32[]{:S(2)}, u32[]{:S(2)}) collective-permute-start(f32[256,256]{0,1:T(8,128)S(1)} %add.59), channel_id=1, source_target_pairs={{0,8},{4,12},{8,0},{12,4},{16,24},{20,28},{24,16},{28,20},{1,9},{5... | collective-permute-start | bytes 786440 | tf_op jit(solution)/shard_map/ppermute | solution.py:9
  58.2 43.4 %collective-permute-start.4 = (f32[256,256]{0,1:T(8,128)S(1)}, f32[256,256]{0,1:T(8,128)S(1)}, u32[]{:S(2)}, u32[]{:S(2)}) collective-permute-start(f32[256,256]{0,1:T(8,128)S(1)} %add.60), channel_id=1, source_target_pairs={{0,16},{4,20},{8,24},{12,28},{16,0},{20,4},{24,8},{28,12},{1,17},{... | collective-permute-start | bytes 786440 | tf_op jit(solution)/shard_map/ppermute | solution.py:9
Sparse Core Ops, SparseCore 0:
  11.4 85.6 all-gather.1
